TPU v7x, 256 devices: a whole 4x4x8 slice. The times are simulated.
256 devices in a mesh: gx: 8 (over y, core), gy: 32 (over x, z).
Axes of the slice: x: 4, y: 4, z: 8, core: 2. Of those that a mesh axis runs over, the one named last changes fastest.
Arguments:
- inputs: bfloat16 [3072, 7168], P('gy', 'gx'), may hold values from -6 to 6
- query_weight: bfloat16 [7168, 7168], P('gy', 'gx'), may hold values from -0.0625 to 0.0625
- key_weight: bfloat16 [7168, 7168], P('gy', 'gx'), may hold values from -0.0625 to 0.0625
- value_weight: bfloat16 [7168, 7168], P('gy', 'gx'), may hold values from -0.0625 to 0.0625
- adapter_down: bfloat16 [128, 7168], P(None, 'gx'), may hold values from -0.0625 to 0.0625
- adapter_up: bfloat16 [7168, 128], P('gy'), may hold values from -0.5 to 0.5
- prompt_keys: bfloat16 [8, 7168, 2048], P('gx', 'gy'), may hold values from -6 to 6
- prompt_values: bfloat16 [8, 7168, 2048], P('gx', 'gy'), may hold values from -6 to 6
- cache_keys: bfloat16 [64, 7168, 512], P('gx', 'gy'), may hold values from -240 to 240
- cache_values: bfloat16 [64, 7168, 512], P('gx', 'gy'), may hold values from -6 to 6
- cache_lengths: int32 [64], P('gx'), may hold values from 1 to 512, as said below
- parents: int32 [64, 48], P('gx'), may hold values from 0 to 46, as said below
- out_weight: bfloat16 [7168, 3584], P('gy', 'gx'), may hold values from -0.125 to 0.125
Outputs:
- layer_output: bfloat16 [3072, 3584], P('gx', 'gy')
Inputs may be any that keep to these rules, and one draw needn't show every extreme that they name: `parents`: node n's parent is a node below n, node 0 is its own parent, and node 47 hangs from node 46. `cache_lengths`: some request has all 512 positions valid.
All inputs are finite; a program needn't handle non-finite values.
Results may differ from a plain program's by a relative error of at most 0.017.
Values may be sent and summed in bfloat16 or wider, within the bound.
No kernel may reach another device: no remote copies, remote signals or barrier semaphores. Data moves between devices by JAX's collectives and lax.ppermute only.
A program may use at most 128 MiB of HBM per device.

v0:
```python
import math
import jax
import jax.numpy as jnp
import numpy as np
from jax import lax
from jax.sharding import Mesh
from jax.sharding import PartitionSpec as P

HEAD = 224
GY = ("gyx", "gyz")


def contract_rows(left, right):
    return lax.dot_general(
        left, right, (((1,), (1,)), ((), ())), preferred_element_type=jnp.float32
    )


def ancestors(parents):
    node_count = parents.shape[1]
    columns = jnp.arange(node_count, dtype=jnp.int32)
    parent_hot = (parents[:, :, None] == columns[None, None, :]).astype(jnp.float32)
    reached = jnp.minimum(jnp.eye(node_count, dtype=jnp.float32)[None] + parent_hot, 1.0)
    rounds = max(1, math.ceil(math.log2(node_count)))
    for sweep in range(rounds):
        reached = jnp.minimum(
            reached + jnp.einsum("rnm,rmk->rnk", reached, reached, precision=lax.Precision.HIGHEST),
            1.0,
        )
    return reached


def attend(queries, new_keys, new_values, prompt_k, prompt_v, cache_k, cache_v, lengths, parents):
    factor = 1.0 / math.sqrt(queries.shape[-1])
    s_prompt = (
        jnp.einsum("rnhe,hep->rnhp", queries, prompt_k, preferred_element_type=jnp.float32) * factor
    )
    s_cache = (
        jnp.einsum("rnhe,rhec->rnhc", queries, cache_k, preferred_element_type=jnp.float32) * factor
    )
    s_tree = (
        jnp.einsum("rnhe,rmhe->rnhm", queries, new_keys, preferred_element_type=jnp.float32)
        * factor
    )
    usable = jnp.arange(cache_k.shape[-1], dtype=jnp.int32)[None, :] < lengths[:, None]
    s_cache = jnp.where(usable[:, None, None, :], s_cache, -jnp.inf)
    reached = ancestors(parents)
    s_tree = jnp.where(reached[:, :, None, :] > 0.5, s_tree, -jnp.inf)
    largest = jnp.maximum(
        jnp.maximum(
            jnp.max(s_prompt, axis=-1, keepdims=True), jnp.max(s_cache, axis=-1, keepdims=True)
        ),
        jnp.max(s_tree, axis=-1, keepdims=True),
    )
    e_prompt = jnp.exp(s_prompt - largest)
    e_cache = jnp.exp(s_cache - largest)
    e_tree = jnp.exp(s_tree - largest)
    totals = (
        jnp.sum(e_prompt, axis=-1, keepdims=True)
        + jnp.sum(e_cache, axis=-1, keepdims=True)
        + jnp.sum(e_tree, axis=-1, keepdims=True)
    )
    w_prompt = (e_prompt / totals).astype(jnp.bfloat16)
    w_cache = (e_cache / totals).astype(jnp.bfloat16)
    w_tree = (e_tree / totals).astype(jnp.bfloat16)
    result = jnp.einsum("rnhp,hep->rnhe", w_prompt, prompt_v, preferred_element_type=jnp.float32)
    result = result + jnp.einsum(
        "rnhc,rhec->rnhe", w_cache, cache_v, preferred_element_type=jnp.float32
    )
    result = result + jnp.einsum(
        "rnhm,rmhe->rnhe", w_tree, new_values, preferred_element_type=jnp.float32
    )
    return result.astype(jnp.bfloat16)


CHUNKS = 1


def gather_like_all_to_all(block, axis_name):
    count = lax.psum(1, axis_name)
    copies = jnp.broadcast_to(block[None], (count,) + block.shape)
    return lax.all_to_all(copies, axis_name, 0, 0, tiled=True)


def per_device(
    inputs,
    query_weight,
    key_weight,
    value_weight,
    adapter_down,
    adapter_up,
    prompt_keys,
    prompt_values,
    cache_keys,
    cache_values,
    cache_lengths,
    parents,
    out_weight,
):
    along_x = lax.psum(1, "gyx")
    along_z = lax.psum(1, "gyz")
    groups = lax.psum(1, "gx")
    node_count = parents.shape[1]
    head_width = query_weight.shape[0]
    head_count = head_width // HEAD
    per_x = groups // along_x
    columns = out_weight.shape[1]
    every_block = gather_like_all_to_all(out_weight, "gx")
    every_block = every_block.reshape(along_x, per_x, head_width, columns)
    own_block = lax.all_to_all(every_block, "gyx", 0, 0, tiled=True)
    folded = jnp.dot(adapter_up, adapter_down, preferred_element_type=jnp.float32)
    folded = (query_weight.astype(jnp.float32) + folded).astype(jnp.bfloat16)
    weights = jnp.concatenate([folded, key_weight, value_weight], axis=0)
    local = inputs.shape[0]
    rows = local // CHUNKS
    results = []
    for chunk in range(CHUNKS):
        piece = inputs[chunk * rows : (chunk + 1) * rows]
        gathered = lax.all_gather(piece, GY, axis=0, tiled=True)
        if chunk == CHUNKS - 1:
            gathered, own_block, weights = lax.optimization_barrier((gathered, own_block, weights))
        mixture = lax.psum_scatter(
            contract_rows(gathered, weights), "gx", scatter_dimension=0, tiled=True
        )
        queries = mixture[:, :head_width].astype(jnp.bfloat16)
        new_keys = mixture[:, head_width : 2 * head_width].astype(jnp.bfloat16)
        new_values = mixture[:, 2 * head_width :].astype(jnp.bfloat16)
        requests = mixture.shape[0] // node_count
        shaped = (requests, node_count, head_count, HEAD)
        cached = (requests, head_count, HEAD, cache_keys.shape[2])
        attended = attend(
            queries.reshape(shaped),
            new_keys.reshape(shaped),
            new_values.reshape(shaped),
            prompt_keys,
            prompt_values,
            cache_keys[chunk::CHUNKS].reshape(cached),
            cache_values[chunk::CHUNKS].reshape(cached),
            cache_lengths[chunk::CHUNKS],
            parents[chunk::CHUNKS],
        )
        flattened = attended.reshape(requests * node_count, head_width)
        heads_along_x = lax.all_gather(flattened, "gyx", axis=1, tiled=True)
        heads_along_x = heads_along_x.reshape(requests * node_count, along_x, head_width)
        partial_sums = jnp.einsum(
            "txe,xkec->tkc", heads_along_x, own_block, preferred_element_type=jnp.float32
        )
        pieces = partial_sums.astype(jnp.bfloat16).reshape(requests * node_count, along_z, -1)
        landed = lax.all_to_all(pieces, "gyz", 1, 1, tiled=True)
        out = jnp.sum(landed.astype(jnp.float32), axis=1).astype(jnp.bfloat16)
        results.append(out.reshape(requests, node_count, -1))
    stacked = jnp.stack(results, axis=1)
    return stacked.reshape(-1, stacked.shape[-1])


def split_mesh(mesh):
    devices = mesh.devices
    along_x = len({d.coords[0] for d in devices[0]})
    shape = (devices.shape[0], along_x, devices.shape[1] // along_x)
    return Mesh(devices.reshape(shape), ("gx",) + GY)


def solution(mesh):
    placed = (
        P(GY, "gx"),
        P(GY, "gx"),
        P(GY, "gx"),
        P(GY, "gx"),
        P(None, "gx"),
        P(GY, None),
        P("gx", GY, None),
        P("gx", GY, None),
        P("gx", GY, None),
        P("gx", GY, None),
        P("gx"),
        P("gx", None),
        P(GY, "gx"),
    )
    return jax.shard_map(
        per_device, mesh=split_mesh(mesh), in_specs=placed, out_specs=P("gx", GY), check_vma=False
    )
```

profile of v0, /device:TPU:8, one launch (start us, length us, event | category | flops | bytes accessed | tf_op | source)
XLA Modules:
  0.0 218.0 jit_solution(15827629615756202001)
XLA Ops:
  6.5 0.7 all-gather.2.cloned.1.call-update
  7.3 1.1 broadcast_in_dim.17
  8.4 28.4 %all_to_all.15 = bf16[8,224,448]{2,1,0:T(8,128)(2,1)} all-to-all(bf16[8,224,448]{2,1,0:T(8,128)(2,1)S(1)} %broadcast_in_dim.17), channel_id=1, replica_groups=mesh['gx'=8,'gyx'=4,'gyz'=8] {'gx'}, dimensions={0} | all-to-all | bytes 3211264 | tf_op jit(solution)/shard_map/all_to_all | solution.py:82
  36.8 4.5 %all-to-all-start.1 = ((bf16[4,2,224,448]{3,2,1,0:T(8,128)(2,1)}), bf16[4,2,224,448]{3,2,1,0:T(8,128)(2,1)}, u32[]{:S(2)}, u32[]{:S(2)}) async-start(bf16[4,2,224,448]{3,2,1,0:T(8,128)(2,1)} %bitcast.120), calls=%async_computation.1 | async-start | bytes 3670016 | tf_op jit(solution)/shard_map/all_to_all | solution.py:110
  41.7 1.1 pad_maximum_fusion
  42.8 22.0 %all-to-all-done.1 = bf16[4,2,224,448]{3,2,1,0:T(8,128)(2,1)} async-done(((bf16[4,2,224,448]{3,2,1,0:T(8,128)(2,1)}), bf16[4,2,224,448]{3,2,1,0:T(8,128)(2,1)}, u32[]{:S(2)}, u32[]{:S(2)}) %all-to-all-start.1) | async-done | bytes 1605664 | tf_op jit(solution)/shard_map/all_to_all | solution.py:110
  64.8 34.1 %all-gather.2.cloned.1.call-done = bf16[3072,896]{1,0:T(8,128)(2,1)} async-done(((bf16[96,896]{1,0:T(8,128)(2,1)}), bf16[3072,896]{1,0:T(8,128)(2,1)}) %all-gather.2.cloned.1.call-update) | async-done | bytes 5505040 | tf_op jit(solution)/shard_map/all_gather | solution.py:119
  98.9 9.2 %fusion.44 = f32[3072,672]{0,1:T(8,128)} fusion(bf16[3072,896]{1,0:T(8,128)(2,1)} %all-gather.2.cloned.1.call-done, bf16[672,896]{1,0:T(8,128)(2,1)S(1)} %pad_maximum_fusion), kind=kOutput, calls=%fused_computation.68 | convolution fusion | flops 3699376128 | bytes 14966784 | tf_op jit(solution)/shard_map/dot_general | solution.py:14
  108.1 0.6 copy-done.8
  108.7 0.4 fusion.15
  109.1 0.3 fusion.16
  109.7 0.3 fusion.18
  110.4 0.3 fusion.24
  110.8 45.9 %reduce-scatter.2.cloned.1.call-done = f32[384,672]{0,1:T(8,128)} async-done(((f32[3072,672]{0,1:T(8,128)}), f32[384,672]{0,1:T(8,128)}) %reduce-scatter.2.cloned.1.call-update) | async-done | bytes 1032208 | tf_op jit(solution)/shard_map/reduce_scatter | solution.py:122
  156.7 1.3 convert.6
  158.4 1.8 bitcast_reduce_fusion
  160.4 0.5 fusion.43
  161.3 0.6 fusion.1
  162.1 3.0 %fusion.9 = f32[8,48,1,224]{3,1,0,2:T(8,128)S(1)} fusion(f32[8,48]{1,0:T(8,128)S(1)} %add_add_fusion, f32[8,48]{1,0:T(8,128)S(1)} %maximum_maximum_fusion, f32[8,48,2048]{2,1,0:T(8,128)} %copy-done.1, bf16[1,224,2048]{2,1,0:T(8,128)(2,1)} %param.20), kind=kOutput, calls=%fused_computation.17 | convolution fusion | flops 354680832 | bytes 4410368 | tf_op jit(solution)/shard_map/rnhp,hep->rnhe/dot_general | solution.py:66
  165.3 0.7 fusion.14
  166.2 14.4 %all_gather.7 = bf16[384,896]{0,1:T(8,128)(2,1)S(1)} all-gather(bf16[384,224]{0,1:T(8,128)(2,1)S(1)} %copy.49), channel_id=1, replica_groups=mesh['gx'=8,'gyx'=4,'gyz'=8] {'gyx'}, dimensions={1}, use_global_device_ids=true | all-gather | bytes 860160 | tf_op jit(solution)/shard_map/all_gather | solution.py:143
  180.6 2.6 %fusion.4 = bf16[384,2,448]{0,2,1:T(8,128)(2,1)S(1)} fusion(bf16[384,4,224,1]{0,2,3,1:T(8,128)(2,1)S(1)} %bitcast.126, bf16[4,2,224,448]{3,2,1,0:T(8,128)(2,1)} %all-to-all-done.1), kind=kOutput, calls=%fused_computation.9 | convolution fusion | flops 616906752 | bytes 2981888 | tf_op jit(solution)/shard_map/txe,xkec->tkc/dot_general | solution.py:145
  183.2 27.2 %all_to_all.16 = bf16[384,8,112]{0,2,1:T(8,128)(2,1)S(1)} all-to-all(bf16[384,8,112]{0,2,1:T(8,128)(2,1)S(1)} %bitcast.125), channel_id=1, replica_groups=mesh['gx'=8,'gyx'=4,'gyz'=8] {'gyz'}, dimensions={1} | all-to-all | bytes 1376256 | tf_op jit(solution)/shard_map/all_to_all | solution.py:149
  210.4 0.7 reduce_sum.42
  (36 shorter events, 2.5 us)
Async XLA Ops:
  6.5 153.9 %copy-start = (bf16[8,224,512]{2,1,0:T(8,128)(2,1)S(1)}, bf16[8,224,512]{2,1,0:T(8,128)(2,1)}, u32[]{:S(2)}) copy-start(bf16[8,224,512]{2,1,0:T(8,128)(2,1)} %param.21) | copy-start | bytes 5505028
  6.5 92.3 %all-gather.2.cloned.1.call-start = ((), (), s32[]{:S(2)}) async-start(), calls=%async_computation.4 | async-start | bytes 5677056 | tf_op jit(solution)/shard_map/all_gather | solution.py:119
  36.8 4.6 %copy-start.3 = (bf16[224,896]{1,0:T(8,128)(2,1)S(1)}, bf16[224,896]{1,0:T(8,128)(2,1)}, u32[]{:S(2)}) copy-start(bf16[224,896]{1,0:T(8,128)(2,1)} %param.14) | copy-start | bytes 1204228
  36.8 4.6 %copy-start.4 = (bf16[128,896]{1,0:T(8,128)(2,1)S(1)}, bf16[128,896]{1,0:T(8,128)(2,1)}, u32[]{:S(2)}) copy-start(bf16[128,896]{1,0:T(8,128)(2,1)} %param.17) | copy-start | bytes 688132
  36.8 4.6 %copy-start.5 = (bf16[224,128]{1,0:T(8,128)(2,1)S(1)}, bf16[224,128]{1,0:T(8,128)(2,1)}, u32[]{:S(2)}) copy-start(bf16[224,128]{1,0:T(8,128)(2,1)} %param.18) | copy-start | bytes 172036
  36.8 4.9 %copy-start.2 = (bf16[224,896]{1,0:T(8,128)(2,1)S(1)}, bf16[224,896]{1,0:T(8,128)(2,1)}, u32[]{:S(2)}) copy-start(bf16[224,896]{1,0:T(8,128)(2,1)} %param.16) | copy-start | bytes 1204228
  36.8 28.0 %all-to-all-start.1 = ((bf16[4,2,224,448]{3,2,1,0:T(8,128)(2,1)}), bf16[4,2,224,448]{3,2,1,0:T(8,128)(2,1)}, u32[]{:S(2)}, u32[]{:S(2)}) async-start(bf16[4,2,224,448]{3,2,1,0:T(8,128)(2,1)} %bitcast.120), calls=%async_computation.1 | async-start | bytes 3670016 | tf_op jit(solution)/shard_map/all_to_all | solution.py:110
  41.3 115.4 %reduce-scatter.2.cloned.1.call-start = ((), (), s32[]{:S(2)}) async-start(), calls=%async_computation.5 | async-start | bytes 9289728 | tf_op jit(solution)/shard_map/reduce_scatter | solution.py:122
  108.0 0.7 copy-start.8
  108.1 2.6 %copy-start.6 = (s32[8]{0:T(128)S(1)}, s32[8]{0:T(128)}, u32[]{:S(2)}) copy-start(s32[8]{0:T(128)} %param.23) | copy-start | bytes 100
  160.2 1.7 copy-start.1
  162.0 3.2 %copy-start.7 = (bf16[8,224,512]{2,1,0:T(8,128)(2,1)S(1)}, bf16[8,224,512]{2,1,0:T(8,128)(2,1)}, u32[]{:S(2)}) copy-start(bf16[8,224,512]{2,1,0:T(8,128)(2,1)} %param.22) | copy-start | bytes 5505028
Sparse Core Ops, SparseCore 0:
  9.9 88.9 all-gather.1
  108.2 48.4 reduce-scatter.1
where the time goes:
time: 218 us
  waiting for transfers between devices  103 us (47%)
  blocking collectives  70 us (32%)
  matrix products  20.5 us (9%)
  between operations  13.7 us (6%)
  starting transfers between devices  4.58 us (2%)
  other arithmetic  4.07 us (2%)
  local copies, waits for them, and re-layouts  2.42 us (1%)
    reduce_scatter x1, waiting for transfers between devices, per_device(): lax.psum_scatter(contract_rows(gathered, weights), 'gx', scatter_dimensio...  45.9 us
    all_gather x1, waiting for transfers between devices, per_device(): gathered = lax.all_gather(piece, GY, axis=0, tiled=True)  34.1 us
    all_to_all x1, blocking collectives, gather_like_all_to_all(): return lax.all_to_all(copies, axis_name, 0, 0, tiled=True)  28.4 us
    all_to_all x1, blocking collectives, per_device(): landed = lax.all_to_all(pieces, 'gyz', 1, 1, tiled=True)  27.2 us
    all_to_all x1, waiting for transfers between devices, per_device(): own_block = lax.all_to_all(every_block, 'gyx', 0, 0, tiled=True)  22 us
    all_gather x1, blocking collectives, per_device(): heads_along_x = lax.all_gather(flattened, 'gyx', axis=1, tiled=True)  14.4 us
    dot_general x1, matrix products, contract_rows(): lax.dot_general(left, right, (((1,), (1,)), ((), ())), preferred_element_...  9.16 us
    all_to_all x1, starting transfers between devices, per_device(): own_block = lax.all_to_all(every_block, 'gyx', 0, 0, tiled=True)  4.54 us
  transfers between devices with their start and end apart: 3, of which 3 were waited for; matrix products, arithmetic and copies ran while one was open for 2% of the time, Pallas kernels for 0%

commit v1 on v0

--- a/solution.py
+++ b/solution.py
@@ -116,7 +116,9 @@
     results = []
     for chunk in range(CHUNKS):
         piece = inputs[chunk * rows : (chunk + 1) * rows]
-        gathered = lax.all_gather(piece, GY, axis=0, tiled=True)
+        gathered = jnp.concatenate(
+            lax.all_to_all(jnp.stack([piece] * lax.axis_size(GY)), GY, 0, 0), axis=0
+        )
         if chunk == CHUNKS - 1:
             gathered, own_block, weights = lax.optimization_barrier((gathered, own_block, weights))
         mixture = lax.psum_scatter(

time: 218 us -> 319 us (1.46)
  waiting for transfers between devices: 103 us -> 168 us
  blocking collectives: 70 us -> 96.9 us
  starting transfers between devices: 4.58 us -> 9.76 us
    all_to_all x1, waiting for transfers between devices: 22 us -> 120 us  [per_device(): lax.all_to_all(jnp.stack([piece] * lax.axis_size(GY)), GY, 0, 0)]
    all_gather x1 -> x0, waiting for transfers between devices: 34.1 us -> none  [per_device(): gathered = lax.all_gather(piece, GY, axis=0, tiled=True)]
    all_to_all x0 -> x1, blocking collectives: none -> 27.5 us  [per_device(): own_block = lax.all_to_all(every_block, 'gyx', 0, 0, tiled=True)]
    all_to_all x1, starting transfers between devices: 4.54 us -> 9.72 us  [per_device(): lax.all_to_all(jnp.stack([piece] * lax.axis_size(GY)), GY, 0, 0)]
  transfers between devices with their start and end apart: 3 -> 2, of which waited for: 3 -> 2; matrix products, arithmetic and copies ran while one was open for 2% -> 1% of each run, Pallas kernels for 0% -> 0%
where the time goes in v1:
time: 319 us; the launch traced here: 318 us
  waiting for transfers between devices  168 us (53%)
  blocking collectives  96.9 us (30%)
  matrix products  20.5 us (6%)
  between operations  13.7 us (4%)
  starting transfers between devices  9.76 us (3%)
  local copies, waits for them, and re-layouts  5.34 us (2%)
  other arithmetic  4.07 us (1%)
    all_to_all x1, waiting for transfers between devices, per_device(): lax.all_to_all(jnp.stack([piece] * lax.axis_size(GY)), GY, 0, 0)  120 us
    reduce_scatter x1, waiting for transfers between devices, per_device(): lax.psum_scatter(contract_rows(gathered, weights), 'gx', scatter_dimensio...  47.9 us
    all_to_all x1, blocking collectives, gather_like_all_to_all(): return lax.all_to_all(copies, axis_name, 0, 0, tiled=True)  27.8 us
    all_to_all x1, blocking collectives, per_device(): own_block = lax.all_to_all(every_block, 'gyx', 0, 0, tiled=True)  27.5 us
    all_to_all x1, blocking collectives, per_device(): landed = lax.all_to_all(pieces, 'gyz', 1, 1, tiled=True)  27.2 us
    all_gather x1, blocking collectives, per_device(): heads_along_x = lax.all_gather(flattened, 'gyx', axis=1, tiled=True)  14.4 us
    all_to_all x1, starting transfers between devices, per_device(): lax.all_to_all(jnp.stack([piece] * lax.axis_size(GY)), GY, 0, 0)  9.72 us
    dot_general x1, matrix products, contract_rows(): lax.dot_general(left, right, (((1,), (1,)), ((), ())), preferred_element_...  9.16 us
  transfers between devices with their start and end apart: 2, of which 2 were waited for; matrix products, arithmetic and copies ran while one was open for 1% of the time, Pallas kernels for 0%

profile of v1, /device:TPU:8, one launch (start us, length us, event | category | flops | bytes accessed | tf_op | source)
XLA Modules:
  0.0 318.2 jit_solution(16721648648887420189)
XLA Ops:
  6.5 1.2 broadcast_in_dim.17
  7.8 27.8 %all_to_all.20 = bf16[8,224,448]{2,1,0:T(8,128)(2,1)S(1)} all-to-all(bf16[8,224,448]{2,1,0:T(8,128)(2,1)S(1)} %broadcast_in_dim.17), channel_id=1, replica_groups=mesh['gx'=8,'gyx'=4,'gyz'=8] {'gx'}, dimensions={0} | all-to-all | bytes 3211264 | tf_op jit(solution)/shard_map/all_to_all | solution.py:82
  35.6 27.5 %all_to_all.21 = bf16[4,2,224,448]{3,2,1,0:T(8,128)(2,1)} all-to-all(bf16[4,2,224,448]{3,2,1,0:T(8,128)(2,1)S(1)} %bitcast.121), channel_id=1, replica_groups=mesh['gx'=8,'gyx'=4,'gyz'=8] {'gyx'}, dimensions={0} | all-to-all | bytes 3211264 | tf_op jit(solution)/shard_map/all_to_all | solution.py:110
  63.1 2.8 stack.2
  65.9 9.7 %all-to-all-start = ((bf16[32,96,896]{2,1,0:T(8,128)(2,1)}), bf16[32,96,896]{2,1,0:T(8,128)(2,1)}, u32[]{:S(2)}, u32[]{:S(2)}) async-start(bf16[32,96,896]{2,1,0:T(8,128)(2,1)} %stack.2), calls=%async_computation | async-start | bytes 11010048 | tf_op jit(solution)/shard_map/all_to_all | solution.py:120
  76.0 1.1 pad_maximum_fusion
  77.1 120.1 %all-to-all-done = bf16[32,96,896]{2,1,0:T(8,128)(2,1)} async-done(((bf16[32,96,896]{2,1,0:T(8,128)(2,1)}), bf16[32,96,896]{2,1,0:T(8,128)(2,1)}, u32[]{:S(2)}, u32[]{:S(2)}) %all-to-all-start) | async-done | bytes 5505056 | tf_op jit(solution)/shard_map/all_to_all | solution.py:120
  197.2 9.2 %fusion.44 = f32[3072,672]{0,1:T(8,128)} fusion(bf16[3072,896]{1,0:T(8,128)(2,1)} %bitcast, bf16[672,896]{1,0:T(8,128)(2,1)S(1)} %pad_maximum_fusion), kind=kOutput, calls=%fused_computation.68 | convolution fusion | flops 3699376128 | bytes 14966784 | tf_op jit(solution)/shard_map/dot_general | solution.py:14
  206.4 0.6 copy-done.9
  207.0 0.4 fusion.15
  207.4 0.3 fusion.16
  208.0 0.3 fusion.18
  208.7 0.3 fusion.24
  209.1 47.9 %reduce-scatter.2.cloned.1.call-done = f32[384,672]{0,1:T(8,128)} async-done(((f32[3072,672]{0,1:T(8,128)}), f32[384,672]{0,1:T(8,128)}) %reduce-scatter.2.cloned.1.call-update) | async-done | bytes 1032208 | tf_op jit(solution)/shard_map/reduce_scatter | solution.py:124
  257.0 1.3 convert.6
  258.6 1.8 bitcast_reduce_fusion
  260.7 0.5 fusion.43
  261.5 0.6 fusion.1
  262.3 3.0 fusion.9
  265.5 0.7 fusion.14
  266.4 14.4 %all_gather.3 = bf16[384,896]{0,1:T(8,128)(2,1)S(1)} all-gather(bf16[384,224]{0,1:T(8,128)(2,1)S(1)} %copy.49), channel_id=1, replica_groups=mesh['gx'=8,'gyx'=4,'gyz'=8] {'gyx'}, dimensions={1}, use_global_device_ids=true | all-gather | bytes 860160 | tf_op jit(solution)/shard_map/all_gather | solution.py:145
  280.8 2.6 fusion.4
  283.5 27.2 %all_to_all.22 = bf16[384,8,112]{0,2,1:T(8,128)(2,1)S(1)} all-to-all(bf16[384,8,112]{0,2,1:T(8,128)(2,1)S(1)} %bitcast.126), channel_id=1, replica_groups=mesh['gx'=8,'gyx'=4,'gyz'=8] {'gyz'}, dimensions={1} | all-to-all | bytes 1376256 | tf_op jit(solution)/shard_map/all_to_all | solution.py:151
  310.7 0.7 reduce_sum.42
  (37 shorter events, 2.5 us)
Async XLA Ops:
  6.5 254.1 %copy-start = (bf16[8,224,512]{2,1,0:T(8,128)(2,1)S(1)}, bf16[8,224,512]{2,1,0:T(8,128)(2,1)}, u32[]{:S(2)}) copy-start(bf16[8,224,512]{2,1,0:T(8,128)(2,1)} %param.21) | copy-start | bytes 5505028
  35.6 27.5 %copy-start.5 = (bf16[96,896]{1,0:T(8,128)(2,1)S(1)}, bf16[96,896]{1,0:T(8,128)(2,1)}, u32[]{:S(2)}) copy-start(bf16[96,896]{1,0:T(8,128)(2,1)} %param.13) | copy-start | bytes 516100
  65.9 9.8 %copy-start.3 = (bf16[224,896]{1,0:T(8,128)(2,1)S(1)}, bf16[224,896]{1,0:T(8,128)(2,1)}, u32[]{:S(2)}) copy-start(bf16[224,896]{1,0:T(8,128)(2,1)} %param.14) | copy-start | bytes 1204228
  65.9 9.8 %copy-start.4 = (bf16[128,896]{1,0:T(8,128)(2,1)S(1)}, bf16[128,896]{1,0:T(8,128)(2,1)}, u32[]{:S(2)}) copy-start(bf16[128,896]{1,0:T(8,128)(2,1)} %param.17) | copy-start | bytes 688132
  65.9 9.8 %copy-start.6 = (bf16[224,128]{1,0:T(8,128)(2,1)S(1)}, bf16[224,128]{1,0:T(8,128)(2,1)}, u32[]{:S(2)}) copy-start(bf16[224,128]{1,0:T(8,128)(2,1)} %param.18) | copy-start | bytes 172036
  65.9 10.1 %copy-start.2 = (bf16[224,896]{1,0:T(8,128)(2,1)S(1)}, bf16[224,896]{1,0:T(8,128)(2,1)}, u32[]{:S(2)}) copy-start(bf16[224,896]{1,0:T(8,128)(2,1)} %param.16) | copy-start | bytes 1204228
  65.9 131.3 %all-to-all-start = ((bf16[32,96,896]{2,1,0:T(8,128)(2,1)}), bf16[32,96,896]{2,1,0:T(8,128)(2,1)}, u32[]{:S(2)}, u32[]{:S(2)}) async-start(bf16[32,96,896]{2,1,0:T(8,128)(2,1)} %stack.2), calls=%async_computation | async-start | bytes 11010048 | tf_op jit(solution)/shard_map/all_to_all | solution.py:120
  75.6 181.3 %reduce-scatter.2.cloned.1.call-start = ((), (), s32[]{:S(2)}) async-start(), calls=%async_computation.5 | async-start | bytes 9289728 | tf_op jit(solution)/shard_map/reduce_scatter | solution.py:124
  206.3 0.7 copy-start.9
  206.4 2.6 copy-start.7
  260.4 1.7 copy-start.1
  262.3 3.2 %copy-start.8 = (bf16[8,224,512]{2,1,0:T(8,128)(2,1)S(1)}, bf16[8,224,512]{2,1,0:T(8,128)(2,1)}, u32[]{:S(2)}) copy-start(bf16[8,224,512]{2,1,0:T(8,128)(2,1)} %param.22) | copy-start | bytes 5505028
Sparse Core Ops, SparseCore 0:
  206.5 50.4 reduce-scatter.1
